TPU v7x, 256 devices: a whole 4x4x8 slice. The times are simulated.
256 devices in a mesh: layer: 64 (over y, z, core), blk: 4 (over x).
Axes of the slice: x: 4, y: 4, z: 8, core: 2. Of those that a mesh axis runs over, the one named last changes fastest.
Arguments:
- mode_matrix: bfloat16 [128, 512, 512], P(None, 'layer', 'blk'), may hold values from -1 to 1, as said below
- decay_rate: bfloat16 [128, 512], P(None, 'layer'), may hold values from 0.0009994507 to 0.29882812
- facet_refl: bfloat16 [128, 512], P(None, 'layer'), may hold values from -0.796875 to 0.796875
Outputs:
- prefix: bfloat16 [64, 4, 512, 512], P('layer', None, 'blk')
Inputs may be any that keep to these rules, and one draw needn't show every extreme that they name: `mode_matrix`: each layer's matrix has orthonormal columns up to the rounding to bfloat16.
All inputs are finite; a program needn't handle non-finite values.
Results may differ from a plain program's by a relative error of at most 0.0045.
The roundings to bfloat16 on the way count: a program that leaves them out, or rounds other values in their place, can miss the bound.
Values may be sent and summed in bfloat16 or wider, within the bound.
No kernel may reach another device: no remote copies, remote signals or barrier semaphores. Data moves between devices by JAX's collectives and lax.ppermute only.
A program may use at most 64 MiB of HBM per device.

v0:
```python
import jax
import jax.numpy as jnp
from jax import lax
from jax.sharding import PartitionSpec as P

HARM = 512
REFL = 4


def passed_along(value, axis, steps):
    count = lax.axis_size(axis)
    first, last = (max(0, -steps), min(count, count - steps))
    return lax.ppermute(value, axis, [(source, source + steps) for source in range(first, last)])


def times_f32(left_op, right_op):
    return jnp.dot(left_op, right_op, preferred_element_type=jnp.float32)


def star_rows(upper_near, upper_far, lower_near, lower_rows):
    coupling_down = times_f32(lower_near[0], upper_far[1]).astype(jnp.bfloat16)
    coupling_up = times_f32(upper_far[1], lower_near[0]).astype(jnp.bfloat16)
    left_sum = upper_near[1]
    for repeat in range(REFL):
        left_sum = (upper_near[1] + times_f32(left_sum, coupling_down)).astype(jnp.bfloat16)
    right_sum = lower_rows[0]
    for repeat in range(REFL):
        right_sum = (lower_rows[0] + times_f32(right_sum, coupling_up)).astype(jnp.bfloat16)
    left_mid = times_f32(left_sum, lower_near[0]).astype(jnp.bfloat16)
    right_mid = times_f32(right_sum, upper_far[1]).astype(jnp.bfloat16)
    new_refl = (upper_near[0] + times_f32(left_mid, upper_far[0])).astype(jnp.bfloat16)
    new_back = times_f32(left_sum, lower_near[1]).astype(jnp.bfloat16)
    new_fore = times_f32(right_sum, upper_far[0]).astype(jnp.bfloat16)
    new_under = (lower_rows[1] + times_f32(right_mid, lower_near[1])).astype(jnp.bfloat16)
    return jnp.stack([new_refl, new_back, new_fore, new_under])


def on_device(mode_matrix, decay_rate, facet_refl):
    relayed_modes, relayed_decay, relayed_refl = (
        lax.all_to_all(mode_matrix, "layer", split_axis=0, concat_axis=1, tiled=True),
        lax.all_to_all(decay_rate, "layer", split_axis=0, concat_axis=1, tiled=True),
        lax.all_to_all(facet_refl, "layer", split_axis=0, concat_axis=1, tiled=True),
    )
    block_index = lax.axis_index("blk")
    row_count = HARM // lax.axis_size("blk")
    row_start = block_index * row_count
    refl_full = relayed_refl.astype(jnp.float32)
    transmit = jnp.sqrt(1.0 - refl_full * refl_full) * jnp.exp(-relayed_decay.astype(jnp.float32))
    mode_piece = lax.all_gather(relayed_modes, "blk", axis=2, tiled=True)
    piece_wide = mode_piece.astype(jnp.float32)
    scaled_refl = (piece_wide * refl_full[:, None, :]).astype(jnp.bfloat16)
    scaled_tran = (piece_wide * transmit[:, None, :]).astype(jnp.bfloat16)
    own_rows = lax.dynamic_slice_in_dim(mode_piece, row_start, row_count, 1)
    refl_part = jnp.einsum(
        "lhm,lkm->lhk", own_rows, scaled_refl, preferred_element_type=jnp.float32
    )
    tran_part = jnp.einsum(
        "lhm,lkm->lhk", own_rows, scaled_tran, preferred_element_type=jnp.float32
    )
    refl_rows = refl_part.astype(jnp.bfloat16)
    tran_rows = tran_part.astype(jnp.bfloat16)
    layer_rows = jnp.stack([refl_rows, tran_rows, tran_rows, -refl_rows], axis=1)
    layer_pair = lax.all_gather(
        jnp.stack([refl_rows, tran_rows], axis=1), "blk", axis=2, tiled=True
    )
    rows_now = layer_rows[0]
    full_now = jnp.stack([layer_pair[0, 0], layer_pair[0, 1], layer_pair[0, 1], -layer_pair[0, 0]])
    rows_now = star_rows(rows_now[0:2], full_now[2:4], layer_pair[1], layer_rows[1, 2:4])
    full_now = lax.all_gather(rows_now, "blk", axis=1, tiled=True)
    group_index = lax.axis_index("layer")
    level_count = lax.axis_size("layer").bit_length() - 1
    for section_level in range(level_count):
        distance = 1 << section_level
        upper_whole = passed_along(full_now, "layer", distance)
        upper_near = lax.dynamic_slice_in_dim(upper_whole[0:2], row_start, row_count, 1)
        upper_far = upper_whole[2:4]
        combined = star_rows(upper_near, upper_far, full_now[0:2], rows_now[2:4])
        rows_now = jnp.where(group_index >= distance, combined, rows_now)
        if section_level + 1 < level_count:
            full_now = lax.all_gather(rows_now, "blk", axis=1, tiled=True)
    return rows_now[None]


def solution(mesh):
    placed = (P(None, "layer", "blk"), P(None, "layer"), P(None, "layer"))
    return jax.shard_map(
        on_device,
        mesh=mesh,
        in_specs=placed,
        out_specs=P("layer", None, "blk", None),
        check_vma=False,
    )
```

profile of v0, /device:TPU:16, one launch (start us, length us, event | category | flops | bytes accessed | tf_op | source)
XLA Modules:
  0.0 783.8 jit_solution(11975169473791905162)
XLA Ops:
  6.5 23.6 %all_to_all.44 = bf16[128,8,128]{2,1,0:T(8,128)(2,1)S(1)} all-to-all(bf16[128,8,128]{2,1,0:T(8,128)(2,1)} %param.3), channel_id=1, replica_groups=mesh['layer'=64,'blk'=4] {'layer'}, dimensions={0} | all-to-all | bytes 524288 | tf_op jit(solution)/shard_map/all_to_all | solution.py:40
  32.3 6.5 all-to-all-start.1
  40.2 6.3 all-to-all-done.1
  46.5 6.4 all-to-all-start.2
  53.1 7.5 all-to-all-done.2
  60.9 1.8 convolution_convert_fusion.15
  62.7 1.8 convolution_convert_fusion.14
  65.5 30.2 %all-gather.11.cloned.1.call-done = bf16[2,2,512,512]{3,2,0,1:T(8,128)(2,1)} async-done(((bf16[2,2,128,512]{3,2,0,1:T(8,128)(2,1)}), bf16[2,2,512,512]{3,2,0,1:T(8,128)(2,1)}) %all-gather.11.cloned.1.call-update) | async-done | bytes 2097168 | tf_op jit(solution)/shard_map/all_gather | solution.py:63
  95.7 1.8 convolution_convert_fusion.12
  101.8 33.5 %all-gather.13.cloned.1.call-done = bf16[4,512,512]{2,1,0:T(8,128)(2,1)} async-done(((bf16[4,128,512]{2,1,0:T(8,128)(2,1)}), bf16[4,512,512]{2,1,0:T(8,128)(2,1)}) %all-gather.13.cloned.1.call-update) | async-done | bytes 2097168 | tf_op jit(solution)/shard_map/all_gather | solution.py:69
  135.3 1.9 collective-permute-start
  137.3 27.7 %collective-permute-done = bf16[4,512,512]{2,1,0:T(8,128)(2,1)S(1)} collective-permute-done((bf16[4,512,512]{2,1,0:T(8,128)(2,1)}, bf16[4,512,512]{2,1,0:T(8,128)(2,1)S(1)}, u32[]{:S(2)}, u32[]{:S(2)}) %collective-permute-start) | collective-permute-done | bytes 2097184 | tf_op jit(solution)/shard_map/ppermute | solution.py:13
  165.0 1.8 convolution_convert_fusion.10
  178.0 32.6 %all-gather.15.cloned.1.call-done = bf16[4,512,512]{2,1,0:T(8,128)(2,1)} async-done(((bf16[4,128,512]{2,1,0:T(8,128)(2,1)}), bf16[4,512,512]{2,1,0:T(8,128)(2,1)}) %all-gather.15.cloned.1.call-update) | async-done | bytes 2097168 | tf_op jit(solution)/shard_map/all_gather | solution.py:80
  210.7 3.5 collective-permute-start.1
  214.1 48.2 %collective-permute-done.1 = bf16[4,512,512]{2,1,0:T(8,128)(2,1)} collective-permute-done((bf16[4,512,512]{2,1,0:T(8,128)(2,1)}, bf16[4,512,512]{2,1,0:T(8,128)(2,1)}, u32[]{:S(2)}, u32[]{:S(2)}) %collective-permute-start.1) | collective-permute-done | bytes 2097184 | tf_op jit(solution)/shard_map/ppermute | solution.py:13
  264.8 1.6 convolution_convert_fusion.9
  275.4 32.6 %all-gather.17.cloned.1.call-done = bf16[4,512,512]{2,1,0:T(8,128)(2,1)} async-done(((bf16[4,128,512]{2,1,0:T(8,128)(2,1)}), bf16[4,512,512]{2,1,0:T(8,128)(2,1)}) %all-gather.17.cloned.1.call-update) | async-done | bytes 2097168 | tf_op jit(solution)/shard_map/all_gather | solution.py:80
  308.1 4.6 collective-permute-start.2
  312.7 93.8 %collective-permute-done.2 = bf16[4,512,512]{2,1,0:T(8,128)(2,1)} collective-permute-done((bf16[4,512,512]{2,1,0:T(8,128)(2,1)}, bf16[4,512,512]{2,1,0:T(8,128)(2,1)}, u32[]{:S(2)}, u32[]{:S(2)}) %collective-permute-start.2) | collective-permute-done | bytes 2097184 | tf_op jit(solution)/shard_map/ppermute | solution.py:13
  406.5 1.6 convolution_convert_fusion.6
  408.9 1.6 convolution_convert_fusion.7
  413.4 1.7 fusion.22
  421.0 32.6 %all-gather.19.cloned.1.call-done = bf16[4,512,512]{2,1,0:T(8,128)(2,1)} async-done(((bf16[4,128,512]{2,1,0:T(8,128)(2,1)}), bf16[4,512,512]{2,1,0:T(8,128)(2,1)}) %all-gather.19.cloned.1.call-update) | async-done | bytes 2097168 | tf_op jit(solution)/shard_map/all_gather | solution.py:80
  453.6 7.6 collective-permute-start.3
  461.3 80.8 %collective-permute-done.3 = bf16[4,512,512]{2,1,0:T(8,128)(2,1)} collective-permute-done((bf16[4,512,512]{2,1,0:T(8,128)(2,1)}, bf16[4,512,512]{2,1,0:T(8,128)(2,1)}, u32[]{:S(2)}, u32[]{:S(2)}) %collective-permute-start.3) | collective-permute-done | bytes 2097184 | tf_op jit(solution)/shard_map/ppermute | solution.py:13
  542.1 1.6 convolution_convert_fusion.4
  549.2 2.0 fusion.55
  551.2 1.7 fusion.27
  554.3 1.7 fusion.114
  559.2 44.1 %all-gather.21.cloned.1.call-done = bf16[4,512,512]{2,1,0:T(8,128)(2,1)} async-done(((bf16[4,128,512]{2,1,0:T(8,128)(2,1)}), bf16[4,512,512]{2,1,0:T(8,128)(2,1)}) %all-gather.21.cloned.1.call-update) | async-done | bytes 2097168 | tf_op jit(solution)/shard_map/all_gather | solution.py:80
  603.4 3.1 collective-permute-start.4
  606.5 46.5 %collective-permute-done.4 = bf16[4,512,512]{2,1,0:T(8,128)(2,1)} collective-permute-done((bf16[4,512,512]{2,1,0:T(8,128)(2,1)}, bf16[4,512,512]{2,1,0:T(8,128)(2,1)}, u32[]{:S(2)}, u32[]{:S(2)}) %collective-permute-start.4) | collective-permute-done | bytes 2097184 | tf_op jit(solution)/shard_map/ppermute | solution.py:13
  652.9 1.6 convolution_convert_fusion.2
  660.1 2.0 fusion.59
  662.0 2.4 fusion.32
  664.4 2.0 convolution_convert_fusion.21
  666.4 2.3 fusion.113
  670.7 2.1 maximum_select_fusion.4
  672.9 33.6 %all-gather.23.cloned.1.call-done = bf16[4,512,512]{2,1,0:T(8,128)(2,1)} async-done(((bf16[4,128,512]{2,1,0:T(8,128)(2,1)}), bf16[4,512,512]{2,1,0:T(8,128)(2,1)}) %all-gather.23.cloned.1.call-update) | async-done | bytes 2097168 | tf_op jit(solution)/shard_map/all_gather | solution.py:80
  707.7 49.8 %collective-permute-done.5 = bf16[4,512,512]{2,1,0:T(8,128)(2,1)} collective-permute-done((bf16[4,512,512]{2,1,0:T(8,128)(2,1)}, bf16[4,512,512]{2,1,0:T(8,128)(2,1)}, u32[]{:S(2)}, u32[]{:S(2)}) %collective-permute-start.5) | collective-permute-done | bytes 2097184 | tf_op jit(solution)/shard_map/ppermute | solution.py:13
  757.5 1.6 convolution_convert_fusion
  760.6 1.6 convolution_convert_fusion.1
  764.6 2.0 fusion.63
  766.6 2.4 fusion.68
  769.0 2.0 fusion.67
  771.0 2.3 fusion.120
  774.7 2.3 maximum_select_fusion.5
  (136 shorter events, 65.1 us)
Async XLA Ops:
  6.5 54.4 %all-gather.9.cloned.1.call-start = ((), (), s32[]{:S(2)}) async-start(), calls=%async_computation.3 | async-start | bytes 1310720 | tf_op jit(solution)/shard_map/all_gather | solution.py:49
  32.3 14.2 %all-to-all-start.1 = ((bf16[64,2,8]{2,1,0:T(2,128)(2,1)}), bf16[64,2,8]{2,1,0:T(2,128)(2,1)S(1)}, u32[]{:S(2)}, u32[]{:S(2)}) async-start(bf16[64,2,8]{2,1,0:T(2,128)(2,1)} %bitcast.3), calls=%async_computation.1 | async-start | bytes 65536 | tf_op jit(solution)/shard_map/all_to_all | solution.py:42
  46.5 14.1 %all-to-all-start.2 = ((bf16[64,2,8]{2,1,0:T(2,128)(2,1)}), bf16[64,2,8]{2,1,0:T(2,128)(2,1)S(1)}, u32[]{:S(2)}, u32[]{:S(2)}) async-start(bf16[64,2,8]{2,1,0:T(2,128)(2,1)} %bitcast.6), calls=%async_computation.2 | async-start | bytes 65536 | tf_op jit(solution)/shard_map/all_to_all | solution.py:41
  52.9 42.8 %all-gather.11.cloned.1.call-start = ((), (), s32[]{:S(2)}) async-start(), calls=%async_computation.4 | async-start | bytes 2621440 | tf_op jit(solution)/shard_map/all_gather | solution.py:63
  65.4 69.9 %all-gather.13.cloned.1.call-start = ((), (), s32[]{:S(2)}) async-start(), calls=%async_computation.5 | async-start | bytes 2621440 | tf_op jit(solution)/shard_map/all_gather | solution.py:69
  95.7 2.6 copy-start.22
  101.7 108.9 %all-gather.15.cloned.1.call-start = ((), (), s32[]{:S(2)}) async-start(), calls=%async_computation.6 | async-start | bytes 2621440 | tf_op jit(solution)/shard_map/all_gather | solution.py:80
  135.3 29.7 %collective-permute-start = (bf16[4,512,512]{2,1,0:T(8,128)(2,1)}, bf16[4,512,512]{2,1,0:T(8,128)(2,1)S(1)}, u32[]{:S(2)}, u32[]{:S(2)}) collective-permute-start(bf16[4,512,512]{2,1,0:T(8,128)(2,1)} %all-gather.13.cloned.1.call-done), channel_id=1, source_target_pairs={{0,4},{4,8},{8,12},{12,16},{16,20},{20,24},{24,28},{28,32},{32,36}... | collective-permute-start | bytes 6291464 | tf_op jit(solution)/shard_map/ppermute | solution.py:13
  165.0 2.7 copy-start.20
  178.0 86.0 %copy-start.1 = (bf16[4,128,512]{2,1,0:T(8,128)(2,1)S(1)}, bf16[4,128,512]{2,1,0:T(8,128)(2,1)}, u32[]{:S(2)}) copy-start(bf16[4,128,512]{2,1,0:T(8,128)(2,1)} %maximum_select_fusion) | copy-start | bytes 1572868
  178.0 130.1 %all-gather.17.cloned.1.call-start = ((), (), s32[]{:S(2)}) async-start(), calls=%async_computation.7 | async-start | bytes 2621440 | tf_op jit(solution)/shard_map/all_gather | solution.py:80
  210.7 51.7 %collective-permute-start.1 = (bf16[4,512,512]{2,1,0:T(8,128)(2,1)}, bf16[4,512,512]{2,1,0:T(8,128)(2,1)}, u32[]{:S(2)}, u32[]{:S(2)}) collective-permute-start(bf16[4,512,512]{2,1,0:T(8,128)(2,1)} %all-gather.15.cloned.1.call-done), channel_id=1, source_target_pairs={{0,8},{4,12},{8,16},{12,20},{16,24},{20,28},{24,32},{28,36},{32,40... | collective-permute-start | bytes 6291464 | tf_op jit(solution)/shard_map/ppermute | solution.py:13
  275.4 132.7 %copy-start.2 = (bf16[4,128,512]{2,1,0:T(8,128)(2,1)S(1)}, bf16[4,128,512]{2,1,0:T(8,128)(2,1)}, u32[]{:S(2)}) copy-start(bf16[4,128,512]{2,1,0:T(8,128)(2,1)} %maximum_select_fusion.1) | copy-start | bytes 1572868
  275.4 178.2 %all-gather.19.cloned.1.call-start = ((), (), s32[]{:S(2)}) async-start(), calls=%async_computation.8 | async-start | bytes 2621440 | tf_op jit(solution)/shard_map/all_gather | solution.py:80
  308.1 98.4 %collective-permute-start.2 = (bf16[4,512,512]{2,1,0:T(8,128)(2,1)}, bf16[4,512,512]{2,1,0:T(8,128)(2,1)}, u32[]{:S(2)}, u32[]{:S(2)}) collective-permute-start(bf16[4,512,512]{2,1,0:T(8,128)(2,1)} %all-gather.17.cloned.1.call-done), channel_id=1, source_target_pairs={{0,16},{4,20},{8,24},{12,28},{16,32},{20,36},{24,40},{28,44},{32,4... | collective-permute-start | bytes 6291464 | tf_op jit(solution)/shard_map/ppermute | solution.py:13
  413.4 2.9 copy-start.21
  419.2 0.7 copy-start.5
  420.9 122.8 %copy-start.3 = (bf16[4,128,512]{2,1,0:T(8,128)(2,1)S(1)}, bf16[4,128,512]{2,1,0:T(8,128)(2,1)}, u32[]{:S(2)}) copy-start(bf16[4,128,512]{2,1,0:T(8,128)(2,1)} %maximum_select_fusion.2) | copy-start | bytes 1572868
  420.9 182.4 %all-gather.21.cloned.1.call-start = ((), (), s32[]{:S(2)}) async-start(), calls=%async_computation.9 | async-start | bytes 2621440 | tf_op jit(solution)/shard_map/all_gather | solution.py:80
  453.6 88.5 %collective-permute-start.3 = (bf16[4,512,512]{2,1,0:T(8,128)(2,1)}, bf16[4,512,512]{2,1,0:T(8,128)(2,1)}, u32[]{:S(2)}, u32[]{:S(2)}) collective-permute-start(bf16[4,512,512]{2,1,0:T(8,128)(2,1)} %all-gather.19.cloned.1.call-done), channel_id=1, source_target_pairs={{0,32},{4,36},{8,40},{12,44},{16,48},{20,52},{24,56},{28,60},{32,6... | collective-permute-start | bytes 6291464 | tf_op jit(solution)/shard_map/ppermute | solution.py:13
  551.2 6.9 copy-start.6
  552.9 6.3 copy-start.9
  554.3 4.9 copy-start.12
  556.0 3.2 copy-start.15
  557.4 0.7 copy-start.18
  559.1 95.4 %copy-start.4 = (bf16[4,128,512]{2,1,0:T(8,128)(2,1)S(1)}, bf16[4,128,512]{2,1,0:T(8,128)(2,1)}, u32[]{:S(2)}) copy-start(bf16[4,128,512]{2,1,0:T(8,128)(2,1)} %maximum_select_fusion.3) | copy-start | bytes 1572868
  559.2 147.3 %all-gather.23.cloned.1.call-start = ((), (), s32[]{:S(2)}) async-start(), calls=%async_computation.10 | async-start | bytes 2621440 | tf_op jit(solution)/shard_map/all_gather | solution.py:80
  603.4 49.6 %collective-permute-start.4 = (bf16[4,512,512]{2,1,0:T(8,128)(2,1)}, bf16[4,512,512]{2,1,0:T(8,128)(2,1)}, u32[]{:S(2)}, u32[]{:S(2)}) collective-permute-start(bf16[4,512,512]{2,1,0:T(8,128)(2,1)} %all-gather.21.cloned.1.call-done), channel_id=1, source_target_pairs={{0,64},{4,68},{8,72},{12,76},{16,80},{20,84},{24,88},{28,92},{32,9... | collective-permute-start | bytes 6291464 | tf_op jit(solution)/shard_map/ppermute | solution.py:13
  662.0 8.7 %copy-start.7 = (bf16[128,512]{1,0:T(8,128)(2,1)S(1)}, bf16[128,512]{1,0:T(8,128)(2,1)}, u32[]{:S(2)}) copy-start(bf16[128,512]{1,0:T(8,128)(2,1)} %copy-done.5) | copy-start | bytes 393220
  662.0 8.7 %copy-start.10 = (bf16[128,512]{1,0:T(8,128)(2,1)S(1)}, bf16[128,512]{1,0:T(8,128)(2,1)}, u32[]{:S(2)}) copy-start(bf16[128,512]{1,0:T(8,128)(2,1)} %copy-done.9) | copy-start | bytes 393220
  662.0 8.7 %copy-start.13 = (bf16[128,512]{1,0:T(8,128)(2,1)S(1)}, bf16[128,512]{1,0:T(8,128)(2,1)}, u32[]{:S(2)}) copy-start(bf16[128,512]{1,0:T(8,128)(2,1)} %copy-done.12) | copy-start | bytes 393220
  662.0 8.7 %copy-start.16 = (bf16[128,512]{1,0:T(8,128)(2,1)S(1)}, bf16[128,512]{1,0:T(8,128)(2,1)}, u32[]{:S(2)}) copy-start(bf16[128,512]{1,0:T(8,128)(2,1)} %copy-done.15) | copy-start | bytes 393220
  670.1 0.7 copy-start.19
  672.8 86.3 %copy-start = (bf16[4,128,512]{2,1,0:T(8,128)(2,1)S(1)}, bf16[4,128,512]{2,1,0:T(8,128)(2,1)}, u32[]{:S(2)}) copy-start(bf16[4,128,512]{2,1,0:T(8,128)(2,1)} %maximum_select_fusion.4) | copy-start | bytes 1572868
  706.4 51.1 %collective-permute-start.5 = (bf16[4,512,512]{2,1,0:T(8,128)(2,1)}, bf16[4,512,512]{2,1,0:T(8,128)(2,1)}, u32[]{:S(2)}, u32[]{:S(2)}) collective-permute-start(bf16[4,512,512]{2,1,0:T(8,128)(2,1)} %all-gather.23.cloned.1.call-done), channel_id=1, source_target_pairs={{0,128},{4,132},{8,136},{12,140},{16,144},{20,148},{24,152},{28,15... | collective-permute-start | bytes 6291464 | tf_op jit(solution)/shard_map/ppermute | solution.py:13
  766.6 8.0 %copy-start.8 = (bf16[128,512]{1,0:T(8,128)(2,1)S(1)}, bf16[128,512]{1,0:T(8,128)(2,1)}, u32[]{:S(2)}) copy-start(bf16[128,512]{1,0:T(8,128)(2,1)} %copy-done.5) | copy-start | bytes 393220
  766.6 8.1 %copy-start.11 = (bf16[128,512]{1,0:T(8,128)(2,1)S(1)}, bf16[128,512]{1,0:T(8,128)(2,1)}, u32[]{:S(2)}) copy-start(bf16[128,512]{1,0:T(8,128)(2,1)} %copy-done.9) | copy-start | bytes 393220
  766.6 8.1 %copy-start.14 = (bf16[128,512]{1,0:T(8,128)(2,1)S(1)}, bf16[128,512]{1,0:T(8,128)(2,1)}, u32[]{:S(2)}) copy-start(bf16[128,512]{1,0:T(8,128)(2,1)} %copy-done.12) | copy-start | bytes 393220
  766.6 8.1 %copy-start.17 = (bf16[128,512]{1,0:T(8,128)(2,1)S(1)}, bf16[128,512]{1,0:T(8,128)(2,1)}, u32[]{:S(2)}) copy-start(bf16[128,512]{1,0:T(8,128)(2,1)} %copy-done.15) | copy-start | bytes 393220
Sparse Core Ops, SparseCore 0:
  31.0 25.5 all-gather.8
  65.5 30.0 all-gather.10
  101.9 33.4 all-gather.12
  178.1 32.5 all-gather.14
  275.5 32.5 all-gather.16
  421.0 32.5 all-gather.18
  559.3 44.0 all-gather.20
  673.0 33.4 all-gather.22
where the time goes:
time: 786 us; the launch traced here: 784 us
  waiting for transfers between devices  600 us (76%)
  matrix products  86.9 us (11%)
  starting transfers between devices  35.1 us (4%)
  blocking collectives  23.6 us (3%)
  between operations  14.3 us (2%)
  local copies, waits for them, and re-layouts  13.7 us (2%)
  other arithmetic  10.2 us (1%)
    ppermute x6, waiting for transfers between devices, passed_along(): lax.ppermute(value, axis, [(source, source + steps) for source in range(f...  347 us
    all_gather x6, waiting for transfers between devices, on_device(): full_now = lax.all_gather(rows_now, 'blk', axis=1, tiled=True)  209 us
    dot_general x70, matrix products, times_f32(): return jnp.dot(left_op, right_op, preferred_element_type=jnp.float32)  83.3 us
    all_gather x1, waiting for transfers between devices, on_device(): lax.all_gather(jnp.stack([refl_rows, tran_rows], axis=1), 'blk', axis=2,...  30.2 us
    all_to_all x1, blocking collectives, on_device(): lax.all_to_all(mode_matrix, 'layer', split_axis=0, concat_axis=1, tiled=T...  23.6 us
    ppermute x6, starting transfers between devices, passed_along(): lax.ppermute(value, axis, [(source, source + steps) for source in range(f...  22 us
  transfers between devices with their start and end apart: 16, of which 15 were waited for; matrix products, arithmetic and copies ran while one was open for 0% of the time, Pallas kernels for 0%

commit v1 on v0

--- a/solution.py
+++ b/solution.py
@@ -5,6 +5,19 @@
 
 HARM = 512
 REFL = 4
+
+
+def pack_case_for(raw):
+    k_now = jnp.concatenate(
+        lax.all_to_all(
+            jnp.stack(jnp.split(raw, lax.axis_size("layer"), 0), 0),
+            concat_axis=0,
+            axis_name="layer",
+            split_axis=0,
+        ),
+        axis=1,
+    )
+    return k_now
 
 
 def passed_along(value, axis, steps):
@@ -37,7 +50,7 @@
 
 def on_device(mode_matrix, decay_rate, facet_refl):
     relayed_modes, relayed_decay, relayed_refl = (
-        lax.all_to_all(mode_matrix, "layer", split_axis=0, concat_axis=1, tiled=True),
+        pack_case_for(mode_matrix),
         lax.all_to_all(decay_rate, "layer", split_axis=0, concat_axis=1, tiled=True),
         lax.all_to_all(facet_refl, "layer", split_axis=0, concat_axis=1, tiled=True),
     )

time: 786 us -> 832 us (1.059)
  local copies, waits for them, and re-layouts: 13.7 us -> 58 us
    unnamed x48 -> x111, local copies, waits for them, and re-layouts: 4.82 us -> 48.5 us
where the time goes in v1:
time: 832 us; the launch traced here: 828 us
  waiting for transfers between devices  600 us (72%)
  matrix products  87 us (10%)
  local copies, waits for them, and re-layouts  58 us (7%)
  starting transfers between devices  35.1 us (4%)
  blocking collectives  23.4 us (3%)
  between operations  14.3 us (2%)
  other arithmetic  10.2 us (1%)
    ppermute x6, waiting for transfers between devices, passed_along(): lax.ppermute(value, axis, [(source, source + steps) for source in range(f...  347 us
    all_gather x6, waiting for transfers between devices, on_device(): full_now = lax.all_gather(rows_now, 'blk', axis=1, tiled=True)  209 us
    dot_general x70, matrix products, times_f32(): return jnp.dot(left_op, right_op, preferred_element_type=jnp.float32)  83.4 us
    unnamed x111, local copies, waits for them, and re-layouts  48.5 us
    all_gather x1, waiting for transfers between devices, on_device(): lax.all_gather(jnp.stack([refl_rows, tran_rows], axis=1), 'blk', axis=2,...  30.2 us
    all_to_all x1, blocking collectives, pack_case_for(): lax.all_to_all(jnp.stack(jnp.split(raw, lax.axis_size('layer'), 0), 0), c...  23.4 us
    ppermute x6, starting transfers between devices, passed_along(): lax.ppermute(value, axis, [(source, source + steps) for source in range(f...  22 us
  transfers between devices with their start and end apart: 16, of which 15 were waited for; matrix products, arithmetic and copies ran while one was open for 0% of the time, Pallas kernels for 0%

profile of v1, /device:TPU:16, one launch (start us, length us, event | category | flops | bytes accessed | tf_op | source)
XLA Modules:
  0.0 828.2 jit_solution(918376820625078141)
XLA Ops:
  50.9 23.4 %all_to_all.31 = bf16[64,2,8,128]{3,2,1,0:T(8,128)(2,1)S(1)} all-to-all(bf16[64,2,8,128]{3,2,1,0:T(8,128)(2,1)S(1)} %constant_dynamic-update-slice_fusion), channel_id=1, replica_groups=mesh['layer'=64,'blk'=4] {'layer'}, dimensions={0} | all-to-all | bytes 524288 | tf_op jit(solution)/shard_map/all_to_all | solution.py:12
  76.5 6.5 all-to-all-start.1
  84.4 6.3 all-to-all-done.1
  90.7 6.4 all-to-all-start.2
  97.3 7.5 all-to-all-done.2
  105.1 1.8 convolution_convert_fusion.15
  106.9 1.8 convolution_convert_fusion.14
  109.7 30.2 %all-gather.11.cloned.1.call-done = bf16[2,2,512,512]{3,2,0,1:T(8,128)(2,1)} async-done(((bf16[2,2,128,512]{3,2,0,1:T(8,128)(2,1)}), bf16[2,2,512,512]{3,2,0,1:T(8,128)(2,1)}) %all-gather.11.cloned.1.call-update) | async-done | bytes 2097168 | tf_op jit(solution)/shard_map/all_gather | solution.py:76
  139.8 1.8 convolution_convert_fusion.12
  146.0 33.5 %all-gather.13.cloned.1.call-done = bf16[4,512,512]{2,1,0:T(8,128)(2,1)} async-done(((bf16[4,128,512]{2,1,0:T(8,128)(2,1)}), bf16[4,512,512]{2,1,0:T(8,128)(2,1)}) %all-gather.13.cloned.1.call-update) | async-done | bytes 2097168 | tf_op jit(solution)/shard_map/all_gather | solution.py:82
  179.5 1.9 collective-permute-start
  181.4 27.7 %collective-permute-done = bf16[4,512,512]{2,1,0:T(8,128)(2,1)S(1)} collective-permute-done((bf16[4,512,512]{2,1,0:T(8,128)(2,1)}, bf16[4,512,512]{2,1,0:T(8,128)(2,1)S(1)}, u32[]{:S(2)}, u32[]{:S(2)}) %collective-permute-start) | collective-permute-done | bytes 2097184 | tf_op jit(solution)/shard_map/ppermute | solution.py:26
  209.2 1.8 convolution_convert_fusion.10
  211.8 1.6 convolution_convert_fusion.11
  222.4 32.6 %all-gather.15.cloned.1.call-done = bf16[4,512,512]{2,1,0:T(8,128)(2,1)} async-done(((bf16[4,128,512]{2,1,0:T(8,128)(2,1)}), bf16[4,512,512]{2,1,0:T(8,128)(2,1)}) %all-gather.15.cloned.1.call-update) | async-done | bytes 2097168 | tf_op jit(solution)/shard_map/all_gather | solution.py:93
  255.0 3.5 collective-permute-start.1
  258.5 48.2 %collective-permute-done.1 = bf16[4,512,512]{2,1,0:T(8,128)(2,1)} collective-permute-done((bf16[4,512,512]{2,1,0:T(8,128)(2,1)}, bf16[4,512,512]{2,1,0:T(8,128)(2,1)}, u32[]{:S(2)}, u32[]{:S(2)}) %collective-permute-start.1) | collective-permute-done | bytes 2097184 | tf_op jit(solution)/shard_map/ppermute | solution.py:26
  309.2 1.6 convolution_convert_fusion.9
  319.8 32.6 %all-gather.17.cloned.1.call-done = bf16[4,512,512]{2,1,0:T(8,128)(2,1)} async-done(((bf16[4,128,512]{2,1,0:T(8,128)(2,1)}), bf16[4,512,512]{2,1,0:T(8,128)(2,1)}) %all-gather.17.cloned.1.call-update) | async-done | bytes 2097168 | tf_op jit(solution)/shard_map/all_gather | solution.py:93
  352.4 4.6 collective-permute-start.2
  357.0 93.8 %collective-permute-done.2 = bf16[4,512,512]{2,1,0:T(8,128)(2,1)} collective-permute-done((bf16[4,512,512]{2,1,0:T(8,128)(2,1)}, bf16[4,512,512]{2,1,0:T(8,128)(2,1)}, u32[]{:S(2)}, u32[]{:S(2)}) %collective-permute-start.2) | collective-permute-done | bytes 2097184 | tf_op jit(solution)/shard_map/ppermute | solution.py:26
  450.8 1.6 convolution_convert_fusion.6
  453.3 1.6 convolution_convert_fusion.7
  457.7 1.7 fusion.22
  465.3 32.6 %all-gather.19.cloned.1.call-done = bf16[4,512,512]{2,1,0:T(8,128)(2,1)} async-done(((bf16[4,128,512]{2,1,0:T(8,128)(2,1)}), bf16[4,512,512]{2,1,0:T(8,128)(2,1)}) %all-gather.19.cloned.1.call-update) | async-done | bytes 2097168 | tf_op jit(solution)/shard_map/all_gather | solution.py:93
  497.9 7.6 collective-permute-start.3
  505.6 80.8 %collective-permute-done.3 = bf16[4,512,512]{2,1,0:T(8,128)(2,1)} collective-permute-done((bf16[4,512,512]{2,1,0:T(8,128)(2,1)}, bf16[4,512,512]{2,1,0:T(8,128)(2,1)}, u32[]{:S(2)}, u32[]{:S(2)}) %collective-permute-start.3) | collective-permute-done | bytes 2097184 | tf_op jit(solution)/shard_map/ppermute | solution.py:26
  586.4 1.6 convolution_convert_fusion.4
  589.5 1.6 convolution_convert_fusion.5
  593.5 2.0 fusion.55
  595.5 1.7 fusion.27
  598.6 1.7 fusion.114
  603.6 44.1 %all-gather.21.cloned.1.call-done = bf16[4,512,512]{2,1,0:T(8,128)(2,1)} async-done(((bf16[4,128,512]{2,1,0:T(8,128)(2,1)}), bf16[4,512,512]{2,1,0:T(8,128)(2,1)}) %all-gather.21.cloned.1.call-update) | async-done | bytes 2097168 | tf_op jit(solution)/shard_map/all_gather | solution.py:93
  647.7 3.1 collective-permute-start.4
  650.8 46.5 %collective-permute-done.4 = bf16[4,512,512]{2,1,0:T(8,128)(2,1)} collective-permute-done((bf16[4,512,512]{2,1,0:T(8,128)(2,1)}, bf16[4,512,512]{2,1,0:T(8,128)(2,1)}, u32[]{:S(2)}, u32[]{:S(2)}) %collective-permute-start.4) | collective-permute-done | bytes 2097184 | tf_op jit(solution)/shard_map/ppermute | solution.py:26
  697.3 1.6 convolution_convert_fusion.2
  704.4 2.0 fusion.59
  706.4 2.4 fusion.32
  708.8 2.0 convolution_convert_fusion.21
  710.8 2.3 fusion.113
  715.1 2.1 maximum_select_fusion.4
  717.2 33.6 %all-gather.23.cloned.1.call-done = bf16[4,512,512]{2,1,0:T(8,128)(2,1)} async-done(((bf16[4,128,512]{2,1,0:T(8,128)(2,1)}), bf16[4,512,512]{2,1,0:T(8,128)(2,1)}) %all-gather.23.cloned.1.call-update) | async-done | bytes 2097168 | tf_op jit(solution)/shard_map/all_gather | solution.py:93
  752.1 49.8 %collective-permute-done.5 = bf16[4,512,512]{2,1,0:T(8,128)(2,1)} collective-permute-done((bf16[4,512,512]{2,1,0:T(8,128)(2,1)}, bf16[4,512,512]{2,1,0:T(8,128)(2,1)}, u32[]{:S(2)}, u32[]{:S(2)}) %collective-permute-start.5) | collective-permute-done | bytes 2097184 | tf_op jit(solution)/shard_map/ppermute | solution.py:26
  809.0 2.0 fusion.63
  811.0 2.4 fusion.68
  813.3 2.0 fusion.67
  815.3 2.3 fusion.120
  819.0 2.3 maximum_select_fusion.5
  (200 shorter events, 109.6 us)
Async XLA Ops:
  6.5 98.6 %all-gather.9.cloned.1.call-start = ((), (), s32[]{:S(2)}) async-start(), calls=%async_computation.3 | async-start | bytes 1310720 | tf_op jit(solution)/shard_map/all_gather | solution.py:62
  76.5 14.2 %all-to-all-start.1 = ((bf16[64,2,8]{2,1,0:T(2,128)(2,1)}), bf16[64,2,8]{2,1,0:T(2,128)(2,1)S(1)}, u32[]{:S(2)}, u32[]{:S(2)}) async-start(bf16[64,2,8]{2,1,0:T(2,128)(2,1)} %bitcast.66), calls=%async_computation.1 | async-start | bytes 65536 | tf_op jit(solution)/shard_map/all_to_all | solution.py:55
  90.7 14.1 %all-to-all-start.2 = ((bf16[64,2,8]{2,1,0:T(2,128)(2,1)}), bf16[64,2,8]{2,1,0:T(2,128)(2,1)S(1)}, u32[]{:S(2)}, u32[]{:S(2)}) async-start(bf16[64,2,8]{2,1,0:T(2,128)(2,1)} %bitcast.69), calls=%async_computation.2 | async-start | bytes 65536 | tf_op jit(solution)/shard_map/all_to_all | solution.py:54
  97.1 42.8 %all-gather.11.cloned.1.call-start = ((), (), s32[]{:S(2)}) async-start(), calls=%async_computation.4 | async-start | bytes 2621440 | tf_op jit(solution)/shard_map/all_gather | solution.py:76
  109.6 69.9 %all-gather.13.cloned.1.call-start = ((), (), s32[]{:S(2)}) async-start(), calls=%async_computation.5 | async-start | bytes 2621440 | tf_op jit(solution)/shard_map/all_gather | solution.py:82
  139.8 2.6 copy-start.22
  145.9 109.1 %all-gather.15.cloned.1.call-start = ((), (), s32[]{:S(2)}) async-start(), calls=%async_computation.6 | async-start | bytes 2621440 | tf_op jit(solution)/shard_map/all_gather | solution.py:93
  179.5 29.7 %collective-permute-start = (bf16[4,512,512]{2,1,0:T(8,128)(2,1)}, bf16[4,512,512]{2,1,0:T(8,128)(2,1)S(1)}, u32[]{:S(2)}, u32[]{:S(2)}) collective-permute-start(bf16[4,512,512]{2,1,0:T(8,128)(2,1)} %all-gather.13.cloned.1.call-done), channel_id=1, source_target_pairs={{0,4},{4,8},{8,12},{12,16},{16,20},{20,24},{24,28},{28,32},{32,36}... | collective-permute-start | bytes 6291464 | tf_op jit(solution)/shard_map/ppermute | solution.py:26
  209.2 2.3 copy-start.20
  222.3 86.0 %copy-start.1 = (bf16[4,128,512]{2,1,0:T(8,128)(2,1)S(1)}, bf16[4,128,512]{2,1,0:T(8,128)(2,1)}, u32[]{:S(2)}) copy-start(bf16[4,128,512]{2,1,0:T(8,128)(2,1)} %maximum_select_fusion) | copy-start | bytes 1572868
  222.3 130.1 %all-gather.17.cloned.1.call-start = ((), (), s32[]{:S(2)}) async-start(), calls=%async_computation.7 | async-start | bytes 2621440 | tf_op jit(solution)/shard_map/all_gather | solution.py:93
  255.0 51.7 %collective-permute-start.1 = (bf16[4,512,512]{2,1,0:T(8,128)(2,1)}, bf16[4,512,512]{2,1,0:T(8,128)(2,1)}, u32[]{:S(2)}, u32[]{:S(2)}) collective-permute-start(bf16[4,512,512]{2,1,0:T(8,128)(2,1)} %all-gather.15.cloned.1.call-done), channel_id=1, source_target_pairs={{0,8},{4,12},{8,16},{12,20},{16,24},{20,28},{24,32},{28,36},{32,40... | collective-permute-start | bytes 6291464 | tf_op jit(solution)/shard_map/ppermute | solution.py:26
  319.7 132.7 %copy-start.2 = (bf16[4,128,512]{2,1,0:T(8,128)(2,1)S(1)}, bf16[4,128,512]{2,1,0:T(8,128)(2,1)}, u32[]{:S(2)}) copy-start(bf16[4,128,512]{2,1,0:T(8,128)(2,1)} %maximum_select_fusion.1) | copy-start | bytes 1572868
  319.7 178.2 %all-gather.19.cloned.1.call-start = ((), (), s32[]{:S(2)}) async-start(), calls=%async_computation.8 | async-start | bytes 2621440 | tf_op jit(solution)/shard_map/all_gather | solution.py:93
  352.4 98.4 %collective-permute-start.2 = (bf16[4,512,512]{2,1,0:T(8,128)(2,1)}, bf16[4,512,512]{2,1,0:T(8,128)(2,1)}, u32[]{:S(2)}, u32[]{:S(2)}) collective-permute-start(bf16[4,512,512]{2,1,0:T(8,128)(2,1)} %all-gather.17.cloned.1.call-done), channel_id=1, source_target_pairs={{0,16},{4,20},{8,24},{12,28},{16,32},{20,36},{24,40},{28,44},{32,4... | collective-permute-start | bytes 6291464 | tf_op jit(solution)/shard_map/ppermute | solution.py:26
  457.7 2.9 copy-start.21
  463.5 0.7 copy-start.5
  465.2 122.8 %copy-start.3 = (bf16[4,128,512]{2,1,0:T(8,128)(2,1)S(1)}, bf16[4,128,512]{2,1,0:T(8,128)(2,1)}, u32[]{:S(2)}) copy-start(bf16[4,128,512]{2,1,0:T(8,128)(2,1)} %maximum_select_fusion.2) | copy-start | bytes 1572868
  465.3 182.4 %all-gather.21.cloned.1.call-start = ((), (), s32[]{:S(2)}) async-start(), calls=%async_computation.9 | async-start | bytes 2621440 | tf_op jit(solution)/shard_map/all_gather | solution.py:93
  497.9 88.5 %collective-permute-start.3 = (bf16[4,512,512]{2,1,0:T(8,128)(2,1)}, bf16[4,512,512]{2,1,0:T(8,128)(2,1)}, u32[]{:S(2)}, u32[]{:S(2)}) collective-permute-start(bf16[4,512,512]{2,1,0:T(8,128)(2,1)} %all-gather.19.cloned.1.call-done), channel_id=1, source_target_pairs={{0,32},{4,36},{8,40},{12,44},{16,48},{20,52},{24,56},{28,60},{32,6... | collective-permute-start | bytes 6291464 | tf_op jit(solution)/shard_map/ppermute | solution.py:26
  595.5 6.9 copy-start.6
  597.2 6.3 copy-start.9
  598.6 4.9 copy-start.12
  600.3 3.2 copy-start.15
  601.7 0.7 copy-start.18
  603.5 95.4 %copy-start.4 = (bf16[4,128,512]{2,1,0:T(8,128)(2,1)S(1)}, bf16[4,128,512]{2,1,0:T(8,128)(2,1)}, u32[]{:S(2)}) copy-start(bf16[4,128,512]{2,1,0:T(8,128)(2,1)} %maximum_select_fusion.3) | copy-start | bytes 1572868
  603.5 147.3 %all-gather.23.cloned.1.call-start = ((), (), s32[]{:S(2)}) async-start(), calls=%async_computation.10 | async-start | bytes 2621440 | tf_op jit(solution)/shard_map/all_gather | solution.py:93
  647.7 49.6 %collective-permute-start.4 = (bf16[4,512,512]{2,1,0:T(8,128)(2,1)}, bf16[4,512,512]{2,1,0:T(8,128)(2,1)}, u32[]{:S(2)}, u32[]{:S(2)}) collective-permute-start(bf16[4,512,512]{2,1,0:T(8,128)(2,1)} %all-gather.21.cloned.1.call-done), channel_id=1, source_target_pairs={{0,64},{4,68},{8,72},{12,76},{16,80},{20,84},{24,88},{28,92},{32,9... | collective-permute-start | bytes 6291464 | tf_op jit(solution)/shard_map/ppermute | solution.py:26
  706.4 8.7 %copy-start.7 = (bf16[128,512]{1,0:T(8,128)(2,1)S(1)}, bf16[128,512]{1,0:T(8,128)(2,1)}, u32[]{:S(2)}) copy-start(bf16[128,512]{1,0:T(8,128)(2,1)} %copy-done.5) | copy-start | bytes 393220
  706.4 8.7 %copy-start.10 = (bf16[128,512]{1,0:T(8,128)(2,1)S(1)}, bf16[128,512]{1,0:T(8,128)(2,1)}, u32[]{:S(2)}) copy-start(bf16[128,512]{1,0:T(8,128)(2,1)} %copy-done.9) | copy-start | bytes 393220
  706.4 8.7 %copy-start.13 = (bf16[128,512]{1,0:T(8,128)(2,1)S(1)}, bf16[128,512]{1,0:T(8,128)(2,1)}, u32[]{:S(2)}) copy-start(bf16[128,512]{1,0:T(8,128)(2,1)} %copy-done.12) | copy-start | bytes 393220
  706.4 8.7 %copy-start.16 = (bf16[128,512]{1,0:T(8,128)(2,1)S(1)}, bf16[128,512]{1,0:T(8,128)(2,1)}, u32[]{:S(2)}) copy-start(bf16[128,512]{1,0:T(8,128)(2,1)} %copy-done.15) | copy-start | bytes 393220
  714.4 0.7 copy-start.19
  717.2 86.3 %copy-start = (bf16[4,128,512]{2,1,0:T(8,128)(2,1)S(1)}, bf16[4,128,512]{2,1,0:T(8,128)(2,1)}, u32[]{:S(2)}) copy-start(bf16[4,128,512]{2,1,0:T(8,128)(2,1)} %maximum_select_fusion.4) | copy-start | bytes 1572868
  750.8 51.1 %collective-permute-start.5 = (bf16[4,512,512]{2,1,0:T(8,128)(2,1)}, bf16[4,512,512]{2,1,0:T(8,128)(2,1)}, u32[]{:S(2)}, u32[]{:S(2)}) collective-permute-start(bf16[4,512,512]{2,1,0:T(8,128)(2,1)} %all-gather.23.cloned.1.call-done), channel_id=1, source_target_pairs={{0,128},{4,132},{8,136},{12,140},{16,144},{20,148},{24,152},{28,15... | collective-permute-start | bytes 6291464 | tf_op jit(solution)/shard_map/ppermute | solution.py:26
  810.9 8.0 copy-start.8
  811.0 8.1 copy-start.11
  811.0 8.1 copy-start.14
  811.0 8.1 copy-start.17
Sparse Core Ops, SparseCore 0:
  75.2 25.5 all-gather.8
  109.7 30.0 all-gather.10
  146.0 33.4 all-gather.12
  222.5 32.5 all-gather.14
  319.8 32.5 all-gather.16
  465.4 32.5 all-gather.18
  603.6 44.0 all-gather.20
  717.3 33.4 all-gather.22
